TPU v7x, 256 devices: a whole 4x4x8 slice. The times are simulated.
256 devices in a mesh: gx: 8 (over x, core), gy: 32 (over y, z).
Axes of the slice: x: 4, y: 4, z: 8, core: 2. Of those that a mesh axis runs over, the one named last changes fastest.
Arguments:
- hidden_in: bfloat16 [8192, 4096], P('gx', 'gy')
- norm_gain: bfloat16 [4096], P('gy'), may hold values from 0.099609375 to 1.8984375
- query_proj: bfloat16 [4096, 4096], P('gx', 'gy')
- kv_proj: bfloat16 [1024, 4096], P(None, 'gy')
- prompt_lengths: int32 [8], replicated, may hold values from 1 to 4096, 8192 in all
- cache_slot: int32 [512], replicated, may hold values from 0 to 511, as said below
Outputs:
- attention: bfloat16 [8192, 4096], P('gy', 'gx')
- kv_cache: bfloat16 [512, 16, 1024], P('gy', None, 'gx')
Inputs may be any that keep to these rules, and one draw needn't show every extreme that they name: `prompt_lengths`: the 8 prompts sum to 8192 tokens; the longest has exactly 4096. `cache_slot`: A permutation of the 512 slots; slot s is held by index s // 16 of gy. The 16 pages of one token block go to any one index at most 1 times, and every index receives exactly 16 pages.
All inputs are finite; a program needn't handle non-finite values.
Results may differ from a plain program's by a relative error of at most 0.0066.
The roundings to bfloat16 on the way count: a program that leaves them out, or rounds other values in their place, can miss the bound.
Values may be sent and summed in bfloat16 or wider, within the bound.
No kernel may reach another device: no remote copies, remote signals or barrier semaphores. Data moves between devices by JAX's collectives and lax.ppermute only.
A program may use at most 128 MiB of HBM per device.

v0:
```python
import math
import jax
import jax.numpy as jnp
from jax import lax
from jax.sharding import PartitionSpec as P

D = 4096
H = 32
KVH = 4
HD = 128
PAGES_DEV = 16
epsilon = 1e-06
rope_base = 5000000.0
masked_out = -1e30


def token_places(prompt_lengths, token_index):
    prompt_ends = jnp.cumsum(prompt_lengths)
    prompt_starts = prompt_ends - prompt_lengths
    segment = jnp.sum((token_index[:, None] >= prompt_ends[None, :]).astype(jnp.int32), axis=1)
    chosen = segment[:, None] == jnp.arange(prompt_lengths.shape[0], dtype=jnp.int32)[None, :]
    opening = jnp.sum(jnp.where(chosen, prompt_starts[None, :], 0), axis=1)
    return (segment, token_index - opening)


def rotate(vectors, places):
    half_size = vectors.shape[-1] // 2
    frequency = rope_base ** (-(jnp.arange(half_size, dtype=jnp.float32) * 2.0) / vectors.shape[-1])
    angles = places.astype(jnp.float32)[:, None] * frequency[None, :]
    cos_part = jnp.cos(angles)[:, None, :]
    sin_part = jnp.sin(angles)[:, None, :]
    leading = vectors[..., :half_size]
    trailing = vectors[..., half_size:]
    return jnp.concatenate(
        [leading * cos_part - trailing * sin_part, trailing * cos_part + leading * sin_part],
        axis=-1,
    )


def local(hidden_in, norm_gain, query_proj, kv_proj, prompt_lengths, cache_slot):
    count_gx = lax.axis_size("gx")
    count_gy = lax.axis_size("gy")
    where_gx = lax.axis_index("gx")
    where_gy = lax.axis_index("gy")
    local_rows = hidden_in.shape[0]
    block_tokens = local_rows * count_gx // count_gy
    all_tokens = block_tokens * count_gy
    heads_here = query_proj.shape[0] // HD
    group_size = H // KVH
    kv_head = where_gx * heads_here // group_size
    contract = (((1,), (1,)), ((), ()))
    kv_width = 2 * HD
    kv_start = kv_head * 2 * HD
    kv_rows = lax.dynamic_slice_in_dim(kv_proj, kv_start, kv_width, 0)
    widened = hidden_in.astype(jnp.float32)
    squares = jnp.sum(widened * widened, axis=1)
    totals = lax.psum(squares, "gy")
    normed = (
        widened * lax.rsqrt(totals / D + epsilon)[:, None] * norm_gain.astype(jnp.float32)[None, :]
    ).astype(jnp.bfloat16)
    gathered = lax.all_gather(normed, "gx", axis=0, tiled=True)
    stacked = jnp.concatenate([query_proj, kv_rows], axis=0)
    projected = lax.psum_scatter(
        lax.dot_general(gathered, stacked, contract, preferred_element_type=jnp.float32),
        "gy",
        scatter_dimension=0,
        tiled=True,
    )
    every_index = jnp.arange(all_tokens, dtype=jnp.int32)
    segment_all, place_all = token_places(prompt_lengths, every_index)
    first_query = where_gy * block_tokens
    token_index = first_query + jnp.arange(block_tokens, dtype=jnp.int32)
    segment_own = lax.dynamic_slice_in_dim(segment_all, first_query, block_tokens, 0)
    place_own = lax.dynamic_slice_in_dim(place_all, first_query, block_tokens, 0)
    query_cols = heads_here * HD
    queries = rotate(
        projected[:, :query_cols].reshape(block_tokens, heads_here, HD), place_own
    ).astype(jnp.bfloat16)
    keys = rotate(projected[:, query_cols : query_cols + HD][:, None, :], place_own)[
        :, 0, :
    ].astype(jnp.bfloat16)
    values = projected[:, query_cols + HD :].astype(jnp.bfloat16)
    cache_cols = jnp.where(where_gx % 2 == 0, keys, values)
    score_scale = 1.0 / math.sqrt(HD)
    last_query = first_query + block_tokens - 1
    first_segment = segment_own[0]
    initial = (
        jnp.full((heads_here, block_tokens), masked_out, jnp.float32),
        jnp.zeros((heads_here, block_tokens), jnp.float32),
        jnp.zeros((heads_here, block_tokens, HD), jnp.float32),
    )
    key_piece = lax.all_gather(keys, "gy", axis=0, tiled=True)
    value_piece = lax.all_gather(values, "gy", axis=0, tiled=True)
    block_count = key_piece.shape[0] // block_tokens
    key_blocks = key_piece.reshape(block_count, block_tokens, HD)
    value_blocks = value_piece.reshape(block_count, block_tokens, HD)

    def one_block(current, inputs):
        key_rows, value_rows, offset = inputs
        block_begin = offset * block_tokens
        key_segment = lax.dynamic_slice_in_dim(segment_all, block_begin, block_tokens, 0)
        skipped = jnp.logical_or(
            block_begin > last_query, key_segment[block_tokens - 1] < first_segment
        )

        def compute(previous):
            running_max, running_sum, running_acc = previous
            key_index = block_begin + jnp.arange(block_tokens, dtype=jnp.int32)
            allowed = (key_segment[None, :] == segment_own[:, None]) & (
                key_index[None, :] <= token_index[:, None]
            )
            scores = (
                jnp.einsum("qhd,kd->hqk", queries, key_rows, preferred_element_type=jnp.float32)
                * score_scale
            )
            scores = jnp.where(allowed[None], scores, masked_out)
            new_max = jnp.maximum(running_max, jnp.max(scores, axis=2))
            weights = jnp.where(allowed[None], jnp.exp(scores - new_max[..., None]), 0.0)
            factor = jnp.exp(running_max - new_max)
            new_sum = running_sum * factor + jnp.sum(weights, axis=2)
            update = jnp.einsum(
                "hqk,kd->hqd",
                weights.astype(jnp.bfloat16),
                value_rows,
                preferred_element_type=jnp.float32,
            )
            return (new_max, new_sum, running_acc * factor[..., None] + update)

        return (lax.cond(skipped, lambda previous: previous, compute, current), None)

    offsets = jnp.arange(block_count, dtype=jnp.int32)
    result, unused = lax.scan(one_block, initial, (key_blocks, value_blocks, offsets))
    final_max, final_sum, final_acc = result
    attention = (
        (final_acc / final_sum[..., None])
        .transpose(1, 0, 2)
        .reshape(block_tokens, query_cols)
        .astype(jnp.bfloat16)
    )
    pages_dev = PAGES_DEV
    page_len = block_tokens // pages_dev
    width_cols = cache_cols.shape[1]
    my_pages = cache_cols.reshape(pages_dev, page_len * width_cols)
    capacity = max(1, pages_dev // count_gy)
    slots_all = count_gy * capacity
    owners = (cache_slot // pages_dev).reshape(count_gy, pages_dev)
    page_range = jnp.arange(pages_dev, dtype=jnp.int32)
    earlier = page_range[None, :] < page_range[:, None]
    same_owner = owners[:, :, None] == owners[:, None, :]
    ranks = jnp.sum((same_owner & earlier[None]).astype(jnp.int32), axis=2)
    my_owner = lax.dynamic_index_in_dim(owners, where_gy, 0, keepdims=False)
    my_rank = lax.dynamic_index_in_dim(ranks, where_gy, 0, keepdims=False)
    target = my_owner * capacity + my_rank
    slot_range = jnp.arange(slots_all, dtype=jnp.int32)
    send_map = (slot_range[:, None] == target[None, :]).astype(jnp.bfloat16)
    outgoing = jnp.dot(send_map, my_pages, preferred_element_type=jnp.float32).astype(jnp.bfloat16)
    incoming = lax.all_to_all(outgoing, "gy", split_axis=0, concat_axis=0, tiled=True)
    wanted = where_gy * pages_dev + page_range
    matches = cache_slot[None, :] == wanted[:, None]
    page_ids = jnp.arange(cache_slot.shape[0], dtype=jnp.int32)
    source_page = jnp.sum(jnp.where(matches, page_ids[None, :], 0), axis=1)
    source_rank = jnp.sum(jnp.where(matches, ranks.reshape(-1)[None, :], 0), axis=1)
    source_slot = source_page // pages_dev * capacity + source_rank
    take_map = (source_slot[:, None] == slot_range[None, :]).astype(jnp.bfloat16)
    cache_block = jnp.dot(take_map, incoming, preferred_element_type=jnp.float32)
    cache_block = cache_block.astype(jnp.bfloat16).reshape(pages_dev, page_len, width_cols)
    return (attention, cache_block)


def solution(mesh):
    return jax.shard_map(
        local,
        mesh=mesh,
        in_specs=(P("gx", "gy"), P("gy"), P("gx", "gy"), P(None, "gy"), P(), P()),
        out_specs=(P("gy", "gx"), P("gy", None, "gx")),
        check_vma=False,
    )
```

profile of v0, /device:TPU:208, one launch (start us, length us, event | category | flops | bytes accessed | tf_op | source)
XLA Modules:
  0.0 692.0 jit_solution(10577667807313542377)
XLA Ops:
  7.2 1.2 fusion.19
  8.4 58.9 %psum.7 = f32[1024]{0:T(1024)S(1)} all-reduce(f32[1024]{0:T(1024)S(1)} %fusion.19), channel_id=1, replica_groups=mesh['gx'=8,'gy'=32] {'gy'}, use_global_device_ids=true, to_apply=%region_1.2 | all-reduce | flops 1024 | bytes 8192 | tf_op jit(solution)/shard_map/psum | solution.py:57
  67.9 1.9 fusion.21
  69.9 38.3 %all-gather.5.cloned.1.call-done = bf16[8192,128]{1,0:T(8,128)(2,1)} async-done(((bf16[1024,128]{1,0:T(8,128)(2,1)}), bf16[8192,128]{1,0:T(8,128)(2,1)}) %all-gather.5.cloned.1.call-update) | async-done | bytes 2097168 | tf_op jit(solution)/shard_map/all_gather | solution.py:61
  108.2 13.3 %fusion.23 = f32[8192,768]{0,1:T(8,128)} fusion(bf16[8192,128]{1,0:T(8,128)(2,1)} %all-gather.5.cloned.1.call-done, bf16[256,128]{1,0:T(8,128)(2,1)S(1)} %constant_dynamic-slice_fusion, bf16[512,128]{1,0:T(8,128)(2,1)} %param.12), kind=kOutput, calls=%fused_computation.42 | convolution fusion | flops 1611005952 | bytes 27459584 | tf_op jit(solution)/shard_map/dot_general | solution.py:64
  122.8 264.6 %reduce-scatter.2.cloned.1.call-done = f32[256,768]{0,1:T(8,128)} async-done(((f32[8192,768]{0,1:T(8,128)}), f32[256,768]{0,1:T(8,128)}) %reduce-scatter.2.cloned.1.call-update) | async-done | bytes 786448 | tf_op jit(solution)/shard_map/reduce_scatter | solution.py:63
  388.8 1.5 bitcast_select_fusion
  395.8 10.1 %all-to-all-start = ((bf16[32,2,1024]{2,1,0:T(2,128)(2,1)}), bf16[32,2,1024]{2,1,0:T(2,128)(2,1)S(1)}, u32[]{:S(2)}, u32[]{:S(2)}) async-start(bf16[32,2,1024]{2,1,0:T(2,128)(2,1)} %reshape.266), calls=%async_computation.1 | async-start | bytes 262144 | tf_op jit(solution)/shard_map/all_to_all | solution.py:157
  406.2 5.9 all-to-all-done
  413.1 52.7 %all-gather.7.cloned.1.call-done = bf16[8192,128]{0,1:T(8,128)(2,1)} async-done(((bf16[256,128]{0,1:T(8,128)(2,1)}), bf16[8192,128]{0,1:T(8,128)(2,1)}) %all-gather.7.cloned.1.call-update) | async-done | bytes 2097168 | tf_op jit(solution)/shard_map/all_gather | solution.py:93
  465.7 3.2 copy.72
  469.0 72.9 %all-gather.9.cloned.1.call-done = bf16[8192,1,128]{0,2,1:T(8,128)(2,1)} async-done(((bf16[256,1,128]{0,2,1:T(8,128)(2,1)}), bf16[8192,1,128]{0,2,1:T(8,128)(2,1)}) %all-gather.9.cloned.1.call-update) | async-done | bytes 2097168 | tf_op jit(solution)/shard_map/all_gather | solution.py:92
  541.8 4.1 copy.71
  546.0 138.6 %while.15 = (s32[]{:T(128)}, f32[4,256]{1,0:T(4,128)S(1)}, f32[4,256]{1,0:T(4,128)S(1)}, f32[4,256,128]{2,1,0:T(8,128)S(1)}, s32[32]{0:T(128)S(1)}, /*index=5*/s...) while((s32[]{:T(128)}, f32[4,256]{1,0:T(4,128)S(1)}, ...), condition=%wide.region_11.12_spmd.clone, body=%wide.region_6.11_spmd.clone.sunk | while | flops 137038352 | bytes 4926361 | solution.py:132
  568.6 2.1 conditional.3
  568.7 1.2 fusion.46
  573.9 2.1 conditional.3
  574.0 1.2 fusion.46
  579.2 2.1 conditional.3
  579.3 1.2 fusion.46
  584.5 2.1 conditional.3
  584.6 1.2 fusion.46
  589.8 2.1 conditional.3
  589.9 1.2 fusion.46
  595.1 2.1 conditional.3
  595.2 1.2 fusion.46
  600.4 2.1 conditional.3
  600.5 1.2 fusion.46
  605.7 2.1 conditional.3
  605.8 1.2 fusion.46
  611.0 2.1 conditional.3
  611.1 1.2 fusion.46
  616.3 2.1 conditional.3
  616.4 1.2 fusion.46
  621.6 2.1 conditional.3
  621.7 1.2 fusion.46
  626.9 2.1 conditional.3
  627.0 1.2 fusion.46
  632.2 2.1 conditional.3
  632.3 1.2 fusion.46
  637.5 2.1 conditional.3
  637.6 1.2 fusion.46
  642.8 2.1 conditional.3
  642.9 1.2 fusion.46
  648.1 2.1 conditional.3
  648.2 1.2 fusion.46
  653.4 2.1 conditional.3
  653.5 1.2 fusion.46
  (353 shorter events, 66.5 us)
Async XLA Ops:
  7.2 62.7 %copy-start = (bf16[1024,128]{1,0:T(8,128)(2,1)S(1)}, bf16[1024,128]{1,0:T(8,128)(2,1)}, u32[]{:S(2)}) copy-start(bf16[1024,128]{1,0:T(8,128)(2,1)} %param.13) | copy-start | bytes 786436
  7.2 101.1 %all-gather.5.cloned.1.call-start = ((), (), s32[]{:S(2)}) async-start(), calls=%async_computation.2 | async-start | bytes 2359296 | tf_op jit(solution)/shard_map/all_gather | solution.py:61
  69.8 317.6 %reduce-scatter.2.cloned.1.call-start = ((), (), s32[]{:S(2)}) async-start(), calls=%async_computation.3 | async-start | bytes 25952256 | tf_op jit(solution)/shard_map/reduce_scatter | solution.py:63
  121.6 0.7 copy-start.2
  121.6 270.1 %copy-start.1 = (s32[512]{0:T(512)S(1)}, s32[512]{0:T(512)}, u32[]{:S(2)}) copy-start(s32[512]{0:T(512)} %param.15) | copy-start | bytes 6148
  121.6 344.1 %all-gather.7.cloned.1.call-start = ((), (), s32[]{:S(2)}) async-start(), calls=%async_computation.4 | async-start | bytes 2162688 | tf_op jit(solution)/shard_map/all_gather | solution.py:93
  387.5 5.6 slice-start
  390.3 151.5 %all-gather.9.cloned.1.call-start = ((), (), s32[]{:S(2)}) async-start(), calls=%async_computation.5 | async-start | bytes 2162688 | tf_op jit(solution)/shard_map/all_gather | solution.py:92
  395.8 16.3 %all-to-all-start = ((bf16[32,2,1024]{2,1,0:T(2,128)(2,1)}), bf16[32,2,1024]{2,1,0:T(2,128)(2,1)S(1)}, u32[]{:S(2)}, u32[]{:S(2)}) async-start(bf16[32,2,1024]{2,1,0:T(2,128)(2,1)} %reshape.266), calls=%async_computation.1 | async-start | bytes 262144 | tf_op jit(solution)/shard_map/all_to_all | solution.py:157
Sparse Core Ops, SparseCore 0:
  69.9 38.2 all-gather.4
  121.7 265.7 reduce-scatter.1
  390.5 75.2 all-gather.6
  468.1 73.7 all-gather.8
where the time goes:
time: 694 us; the launch traced here: 692 us
  waiting for transfers between devices  434 us (63%)
  loops' own time  63.5 us (9%)
  blocking collectives  58.9 us (8%)
  local copies, waits for them, and re-layouts  52.8 us (8%)
  matrix products  42.2 us (6%)
  other arithmetic  16 us (2%)
  between operations  14 us (2%)
  starting transfers between devices  10.3 us (1%)
    reduce_scatter x1, waiting for transfers between devices, local(): lax.psum_scatter(lax.dot_general(gathered, stacked, contract, preferred_e...  265 us
    all_gather x1, waiting for transfers between devices, local(): key_piece = lax.all_gather(keys, 'gy', axis=0, tiled=True)  72.9 us
    another operation x1, loops' own time, local(): lax.scan(one_block, initial, (key_blocks, value_blocks, offsets))  62.1 us
    psum x1, blocking collectives, local(): totals = lax.psum(squares, 'gy')  58.9 us
    all_gather x1, waiting for transfers between devices, local(): value_piece = lax.all_gather(values, 'gy', axis=0, tiled=True)  52.7 us
    all_gather x1, waiting for transfers between devices, local(): gathered = lax.all_gather(normed, 'gx', axis=0, tiled=True)  38.3 us
    dot_general x17, matrix products, compute(): jnp.einsum('qhd,kd->hqk', queries, key_rows, preferred_element_type=jnp.f...  19.9 us
    slice x32, local copies, waits for them, and re-layouts, one_block(): key_segment[block_tokens - 1] < first_segment  18.9 us
  transfers between devices with their start and end apart: 5, of which 5 were waited for; matrix products, arithmetic and copies ran while one was open for 1% of the time, Pallas kernels for 0%

commit v1 on v0

--- a/solution.py
+++ b/solution.py
@@ -54,7 +54,9 @@
     kv_rows = lax.dynamic_slice_in_dim(kv_proj, kv_start, kv_width, 0)
     widened = hidden_in.astype(jnp.float32)
     squares = jnp.sum(widened * widened, axis=1)
-    totals = lax.psum(squares, "gy")
+    totals = squares
+    for hop in (1, 2, 4, 8, 16):
+        totals = totals + lax.ppermute(totals, "gy", [(dev, dev ^ hop) for dev in range(32)])
     normed = (
         widened * lax.rsqrt(totals / D + epsilon)[:, None] * norm_gain.astype(jnp.float32)[None, :]
     ).astype(jnp.bfloat16)

time: 694 us -> 651 us (0.938)
  blocking collectives: 58.9 us -> 0 us
  waiting for transfers between devices: 434 us -> 444 us
    psum x1 -> x0, blocking collectives: 58.9 us -> none  [local(): totals = lax.psum(squares, 'gy')]
    ppermute x0 -> x5, waiting for transfers between devices: none -> 19 us  [local(): lax.ppermute(totals, 'gy', [(dev, dev ^ hop) for dev in range(32)])]
    all_gather x1, waiting for transfers between devices: 38.3 us -> 28.5 us  [local(): gathered = lax.all_gather(normed, 'gx', axis=0, tiled=True)]
  transfers between devices with their start and end apart: 5 -> 10, of which waited for: 5 -> 10; matrix products, arithmetic and copies ran while one was open for 1% -> 2% of each run, Pallas kernels for 0% -> 0%
where the time goes in v1:
time: 651 us; the launch traced here: 649 us
  waiting for transfers between devices  444 us (68%)
  loops' own time  65.2 us (10%)
  local copies, waits for them, and re-layouts  52.8 us (8%)
  matrix products  42.2 us (6%)
  other arithmetic  16 us (2%)
  starting transfers between devices  14.9 us (2%)
  between operations  14 us (2%)
    reduce_scatter x1, waiting for transfers between devices, local(): lax.psum_scatter(lax.dot_general(gathered, stacked, contract, preferred_e...  265 us
    all_gather x1, waiting for transfers between devices, local(): key_piece = lax.all_gather(keys, 'gy', axis=0, tiled=True)  72.9 us
    another operation x1, loops' own time, local(): lax.scan(one_block, initial, (key_blocks, value_blocks, offsets))  63.9 us
    all_gather x1, waiting for transfers between devices, local(): value_piece = lax.all_gather(values, 'gy', axis=0, tiled=True)  52.9 us
    all_gather x1, waiting for transfers between devices, local(): gathered = lax.all_gather(normed, 'gx', axis=0, tiled=True)  28.5 us
    dot_general x17, matrix products, compute(): jnp.einsum('qhd,kd->hqk', queries, key_rows, preferred_element_type=jnp.f...  19.9 us
    ppermute x5, waiting for transfers between devices, local(): lax.ppermute(totals, 'gy', [(dev, dev ^ hop) for dev in range(32)])  19 us
    slice x32, local copies, waits for them, and re-layouts, one_block(): key_segment[block_tokens - 1] < first_segment  18.9 us
  transfers between devices with their start and end apart: 10, of which 10 were waited for; matrix products, arithmetic and copies ran while one was open for 2% of the time, Pallas kernels for 0%

profile of v1, /device:TPU:208, one launch (start us, length us, event | category | flops | bytes accessed | tf_op | source)
XLA Modules:
  0.0 649.1 jit_solution(1689336288383197106)
XLA Ops:
  7.2 1.2 fusion.19
  9.5 2.6 collective-permute-done
  12.1 1.5 collective-permute-start.1
  13.6 3.1 collective-permute-done.1
  17.2 7.0 %collective-permute-done.2 = f32[1024]{0:T(1024)S(1)} collective-permute-done((f32[1024]{0:T(1024)S(1)}, f32[1024]{0:T(1024)S(1)}, u32[]{:S(2)}, u32[]{:S(2)}) %collective-permute-start.2) | collective-permute-done | bytes 4128 | tf_op jit(solution)/shard_map/ppermute | solution.py:59
  24.2 1.3 collective-permute-start.3
  25.4 2.3 collective-permute-done.3
  28.8 4.1 collective-permute-done.4
  32.9 1.9 fusion.21
  34.9 28.5 %all-gather.5.cloned.1.call-done = bf16[8192,128]{1,0:T(8,128)(2,1)} async-done(((bf16[1024,128]{1,0:T(8,128)(2,1)}), bf16[8192,128]{1,0:T(8,128)(2,1)}) %all-gather.5.cloned.1.call-update) | async-done | bytes 2097168 | tf_op jit(solution)/shard_map/all_gather | solution.py:63
  63.4 13.3 %fusion.23 = f32[8192,768]{0,1:T(8,128)} fusion(bf16[8192,128]{1,0:T(8,128)(2,1)} %all-gather.5.cloned.1.call-done, bf16[256,128]{1,0:T(8,128)(2,1)S(1)} %constant_dynamic-slice_fusion, bf16[512,128]{1,0:T(8,128)(2,1)} %param.12), kind=kOutput, calls=%fused_computation.42 | convolution fusion | flops 1611005952 | bytes 27459584 | tf_op jit(solution)/shard_map/dot_general | solution.py:66
  77.9 264.8 %reduce-scatter.2.cloned.1.call-done = f32[256,768]{0,1:T(8,128)} async-done(((f32[8192,768]{0,1:T(8,128)}), f32[256,768]{0,1:T(8,128)}) %reduce-scatter.2.cloned.1.call-update) | async-done | bytes 786448 | tf_op jit(solution)/shard_map/reduce_scatter | solution.py:65
  344.0 1.5 bitcast_select_fusion
  351.1 10.0 %all-to-all-start = ((bf16[32,2,1024]{2,1,0:T(2,128)(2,1)}), bf16[32,2,1024]{2,1,0:T(2,128)(2,1)S(1)}, u32[]{:S(2)}, u32[]{:S(2)}) async-start(bf16[32,2,1024]{2,1,0:T(2,128)(2,1)} %reshape.266), calls=%async_computation.1 | async-start | bytes 262144 | tf_op jit(solution)/shard_map/all_to_all | solution.py:159
  361.4 5.8 all-to-all-done
  368.2 52.9 %all-gather.7.cloned.1.call-done = bf16[8192,128]{0,1:T(8,128)(2,1)} async-done(((bf16[256,128]{0,1:T(8,128)(2,1)}), bf16[8192,128]{0,1:T(8,128)(2,1)}) %all-gather.7.cloned.1.call-update) | async-done | bytes 2097168 | tf_op jit(solution)/shard_map/all_gather | solution.py:95
  421.1 3.2 copy.72
  424.3 72.9 %all-gather.9.cloned.1.call-done = bf16[8192,1,128]{0,2,1:T(8,128)(2,1)} async-done(((bf16[256,1,128]{0,2,1:T(8,128)(2,1)}), bf16[8192,1,128]{0,2,1:T(8,128)(2,1)}) %all-gather.9.cloned.1.call-update) | async-done | bytes 2097168 | tf_op jit(solution)/shard_map/all_gather | solution.py:94
  497.2 4.1 copy.71
  501.3 140.3 %while.15 = (s32[]{:T(128)}, f32[4,256]{1,0:T(4,128)S(1)}, f32[4,256]{1,0:T(4,128)S(1)}, f32[4,256,128]{2,1,0:T(8,128)S(1)}, s32[32]{0:T(128)S(1)}, /*index=5*/s...) while((s32[]{:T(128)}, f32[4,256]{1,0:T(4,128)S(1)}, ...), condition=%wide.region_10.11_spmd.clone, body=%wide.region_5.10_spmd.clone.sunk | while | flops 137038352 | bytes 4926361 | solution.py:134
  524.3 2.1 conditional.3
  524.4 1.2 fusion.46
  529.6 2.1 conditional.3
  529.8 1.2 fusion.46
  535.0 2.1 conditional.3
  535.1 1.2 fusion.46
  540.3 2.1 conditional.3
  540.5 1.2 fusion.46
  545.7 2.1 conditional.3
  545.9 1.2 fusion.46
  551.0 2.1 conditional.3
  551.2 1.2 fusion.46
  556.4 2.1 conditional.3
  556.6 1.2 fusion.46
  561.8 2.1 conditional.3
  567.1 2.1 conditional.3
  572.5 2.1 conditional.3
  577.8 2.1 conditional.3
  578.0 1.2 fusion.46
  583.2 2.1 conditional.3
  588.5 2.1 conditional.3
  588.7 1.2 fusion.46
  593.9 2.1 conditional.3
  599.2 2.1 conditional.3
  599.4 1.2 fusion.46
  604.6 2.1 conditional.3
  610.0 2.1 conditional.3
  610.1 1.2 fusion.46
  (366 shorter events, 75.6 us)
Async XLA Ops:
  7.2 27.7 %copy-start = (bf16[1024,128]{1,0:T(8,128)(2,1)S(1)}, bf16[1024,128]{1,0:T(8,128)(2,1)}, u32[]{:S(2)}) copy-start(bf16[1024,128]{1,0:T(8,128)(2,1)} %param.13) | copy-start | bytes 786436
  7.2 56.2 %all-gather.5.cloned.1.call-start = ((), (), s32[]{:S(2)}) async-start(), calls=%async_computation.2 | async-start | bytes 2359296 | tf_op jit(solution)/shard_map/all_gather | solution.py:63
  8.4 3.7 collective-permute-start
  12.1 4.5 collective-permute-start.1
  16.6 7.5 %collective-permute-start.2 = (f32[1024]{0:T(1024)S(1)}, f32[1024]{0:T(1024)S(1)}, u32[]{:S(2)}, u32[]{:S(2)}) collective-permute-start(f32[1024]{0:T(1024)S(1)} %add.115), channel_id=1, source_target_pairs={{0,4},{1,5},{2,6},{3,7},{4,0},{5,1},{6,2},{7,3},{8,12},{9,13},{10,... | collective-permute-start | bytes 12296 | tf_op jit(solution)/shard_map/ppermute | solution.py:59
  24.2 3.6 collective-permute-start.3
  27.8 5.1 collective-permute-start.4
  34.8 308.0 %reduce-scatter.2.cloned.1.call-start = ((), (), s32[]{:S(2)}) async-start(), calls=%async_computation.3 | async-start | bytes 25952256 | tf_op jit(solution)/shard_map/reduce_scatter | solution.py:65
  76.7 0.7 copy-start.2
  76.7 270.3 %copy-start.1 = (s32[512]{0:T(512)S(1)}, s32[512]{0:T(512)}, u32[]{:S(2)}) copy-start(s32[512]{0:T(512)} %param.15) | copy-start | bytes 6148
  76.7 344.4 %all-gather.7.cloned.1.call-start = ((), (), s32[]{:S(2)}) async-start(), calls=%async_computation.4 | async-start | bytes 2162688 | tf_op jit(solution)/shard_map/all_gather | solution.py:95
  342.7 5.6 slice-start
  345.6 151.6 %all-gather.9.cloned.1.call-start = ((), (), s32[]{:S(2)}) async-start(), calls=%async_computation.5 | async-start | bytes 2162688 | tf_op jit(solution)/shard_map/all_gather | solution.py:94
  351.1 16.2 %all-to-all-start = ((bf16[32,2,1024]{2,1,0:T(2,128)(2,1)}), bf16[32,2,1024]{2,1,0:T(2,128)(2,1)S(1)}, u32[]{:S(2)}, u32[]{:S(2)}) async-start(bf16[32,2,1024]{2,1,0:T(2,128)(2,1)} %reshape.266), calls=%async_computation.1 | async-start | bytes 262144 | tf_op jit(solution)/shard_map/all_to_all | solution.py:159
Sparse Core Ops, SparseCore 0:
  34.9 28.4 all-gather.4
  76.8 265.8 reduce-scatter.1
  345.7 75.3 all-gather.6
  423.4 73.7 all-gather.8
